TPU v7x, 256 devices: a whole 4x4x8 slice. The times are simulated.
256 devices in a mesh: cfg: 2 (over core), req: 8 (over z), seq: 16 (over y, x).
Axes of the slice: x: 4, y: 4, z: 8, core: 2. Of those that a mesh axis runs over, the one named last changes fastest.
Arguments:
- img_hidden: bfloat16 [2, 16, 512, 1536], P('cfg', 'req', 'seq'), may hold values from -6 to 6
- txt_hidden: bfloat16 [2, 16, 160, 1536], P('cfg', 'req', 'seq'), may hold values from -6 to 6
- text_len: int32 [2, 16], P('cfg'), may hold values from 1 to 154, as said below
- pooled: float32 [2, 16, 1536], P('cfg'), may hold values from -6 to 6
- timestep: int32 [16], replicated, may hold values from 0 to 27
- latent: float32 [16, 512, 64], P('req', 'seq', 'cfg'), may hold values from -24 to 24
- mod_weight: bfloat16 [1536, 15360], P(None, ('req', 'seq')), may hold values from -0.15625 to 0.15625
- mod_bias: float32 [15360], P(('req', 'seq')), may hold values from -2 to 2
- img_qkv: bfloat16 [1536, 3, 1536], P(None, None, 'req'), may hold values from -2.5 to 2.5
- txt_kv: bfloat16 [1536, 2, 1536], P(None, None, 'req'), may hold values from -0.15625 to 0.15625
- out_weight: bfloat16 [1536, 1536], P('req'), may hold values from -0.15625 to 0.15625
- fc_in: bfloat16 [1536, 6144], P(None, 'seq'), may hold values from -0.15625 to 0.15625
- fc_out: bfloat16 [6144, 1536], P('seq'), may hold values from -0.078125 to 0.078125
- final_weight: bfloat16 [1536, 64], replicated, may hold values from -0.15625 to 0.15625
Outputs:
- velocity: float32 [16, 512, 64], P('req', 'seq', 'cfg')
- next_latent: float32 [16, 512, 64], P('req', 'seq', 'cfg')
- latent_norm: float32 [16], P('req')
- latent_peak: float32 [16], P('req')
Inputs may be any that keep to these rules, and one draw needn't show every extreme that they name: Text slots from text_len to 159 of a request are padding; every draw has a request of length 154 and one of length 1.
All inputs are finite; a program needn't handle non-finite values.
Results may differ from a plain program's by a relative error of at most 0.015.
Values may be sent and summed in bfloat16 or wider, within the bound.
No kernel may reach another device: no remote copies, remote signals or barrier semaphores. Data moves between devices by JAX's collectives and lax.ppermute only.
A program may use at most 64 MiB of HBM per device.

v0:
```python
import math

import jax
import jax.numpy as jnp
from jax import lax
from jax.sharding import PartitionSpec as P

D = 1536
HD = 64
PATCHC = 64
IMG = 512
STEPS = 28


SIGMA_SHIFT = 3.0
GUIDANCE = 5.0
EPSILON = 1e-06
MASKED_SCORE = -1e30


def from_partner(value, axis, distance):
    mask = 2**distance
    pairs = [(source, source ^ mask) for source in range(lax.axis_size(axis))]
    return lax.ppermute(value, axis, pairs)


def shifted(fraction):
    return SIGMA_SHIFT * fraction / (1.0 + (SIGMA_SHIFT - 1.0) * fraction)


def plan(timestep):
    position = timestep.astype(jnp.float32)
    return (shifted(1.0 - position / STEPS), shifted(1.0 - (position + 1.0) / STEPS))


def time_features(sigma):
    half_width = D // 2
    frequency = jnp.exp(-math.log(10000.0) * jnp.arange(half_width, dtype=jnp.float32) / half_width)
    angles = (1000.0 * sigma)[:, None] * frequency[None, :]
    return jnp.concatenate([jnp.cos(angles), jnp.sin(angles)], axis=1)


def layer_norm(values):
    average = jnp.mean(values, axis=-1, keepdims=True)
    centred = values - average
    spread = jnp.mean(centred * centred, axis=-1, keepdims=True)
    return centred * lax.rsqrt(spread + EPSILON)


def attention(queries, key_rows, value_rows, live_keys):
    query_count = queries.shape[0]
    head_count = queries.shape[1]
    block_rows = min(512, query_count)
    scale_factor = HD ** (-0.5)

    def one_block(query_block):
        scores = (
            jnp.einsum("qhd,khd->hqk", query_block, key_rows, preferred_element_type=jnp.float32)
            * scale_factor
        )
        scores = jnp.where(live_keys[None, None, :], scores, MASKED_SCORE)
        highest = jnp.max(scores, axis=-1, keepdims=True)
        exp_scores = jnp.exp(scores - highest)
        weights = (exp_scores / jnp.sum(exp_scores, axis=-1, keepdims=True)).astype(jnp.bfloat16)
        mixture = jnp.einsum(
            "hqk,khd->qhd", weights, value_rows, preferred_element_type=jnp.float32
        )
        return mixture.astype(jnp.bfloat16)

    blocks = queries.reshape(query_count // block_rows, block_rows, head_count, HD)
    return lax.map(one_block, blocks).reshape(query_count, head_count * HD)


def on_device(
    img_hidden,
    txt_hidden,
    text_len,
    pooled,
    timestep,
    latent,
    mod_weight,
    mod_bias,
    img_qkv,
    txt_kv,
    out_weight,
    fc_in,
    fc_out,
    final_weight,
):
    group_size = img_hidden.shape[1]
    current, upcoming = plan(timestep)
    activated = jax.nn.silu(pooled[0] + time_features(current)).astype(jnp.bfloat16)
    columns = jnp.dot(activated, mod_weight, preferred_element_type=jnp.float32) + mod_bias
    every_mod = lax.all_gather(columns, ("req", "seq"), axis=1, tiled=True)
    offset = lax.axis_index("req") * group_size
    modulation = lax.dynamic_slice_in_dim(every_mod, offset, group_size, 0).reshape(
        group_size, 10, 1, D
    )
    shift_attn, scale_attn, gate_attn = (modulation[:, 0], modulation[:, 1], modulation[:, 2])
    shift_mlp, scale_mlp, gate_mlp = (modulation[:, 3], modulation[:, 4], modulation[:, 5])
    shift_text, scale_text = (modulation[:, 6], modulation[:, 7])
    scale_final, shift_final = (modulation[:, 8], modulation[:, 9])
    img_float = img_hidden[0].astype(jnp.float32)
    img_in = (layer_norm(img_float) * (1.0 + scale_attn) + shift_attn).astype(jnp.bfloat16)
    txt_in = (
        layer_norm(txt_hidden[0].astype(jnp.float32)) * (1.0 + scale_text) + shift_text
    ).astype(jnp.bfloat16)
    all_img, all_txt = (
        lax.all_gather(img_in, "req", axis=0, tiled=True),
        lax.all_gather(txt_in, "req", axis=0, tiled=True),
    )
    head_width = img_qkv.shape[2]
    local_heads = head_width // HD
    qkv_columns = img_qkv.reshape(D, 3 * head_width)
    kv_columns = txt_kv.reshape(D, 2 * head_width)
    own_img, own_txt = (
        lax.all_to_all(all_img, "seq", split_axis=0, concat_axis=1, tiled=True),
        lax.all_to_all(all_txt, "seq", split_axis=0, concat_axis=1, tiled=True),
    )
    own_proj = jnp.einsum(
        "rnd,dc->rnc", own_img, qkv_columns, preferred_element_type=jnp.float32
    ).astype(jnp.bfloat16)
    own_proj_txt = jnp.einsum(
        "rnd,dc->rnc", own_txt, kv_columns, preferred_element_type=jnp.float32
    ).astype(jnp.bfloat16)
    local_count = own_proj.shape[0]
    image_rows = own_proj.shape[1]
    text_rows = own_proj_txt.shape[1]
    first_request = lax.axis_index("seq") * local_count

    def attend_request(operands):
        projected, projected_txt, request_slot = operands
        queries = projected[:, :head_width]
        key_rows = jnp.concatenate(
            [projected[:, head_width : 2 * head_width], projected_txt[:, :head_width]], axis=0
        )
        value_rows = jnp.concatenate(
            [projected[:, 2 * head_width :], projected_txt[:, head_width:]], axis=0
        )
        text_count = lax.dynamic_index_in_dim(text_len[0], first_request + request_slot, 0, False)
        live_keys = jnp.arange(image_rows + text_rows, dtype=jnp.int32) < image_rows + text_count
        total_keys = image_rows + text_rows
        return attention(
            queries.reshape(image_rows, local_heads, HD),
            key_rows.reshape(total_keys, local_heads, HD),
            value_rows.reshape(total_keys, local_heads, HD),
            live_keys,
        )

    attended = lax.map(
        attend_request, (own_proj, own_proj_txt, jnp.arange(local_count, dtype=jnp.int32))
    )
    projected_rows = jnp.einsum(
        "rnk,kd->rnd", attended, out_weight, preferred_element_type=jnp.float32
    )
    moved_rows = lax.all_to_all(
        projected_rows.astype(jnp.bfloat16), "seq", split_axis=1, concat_axis=0, tiled=True
    ).astype(projected_rows.dtype)
    attn_out = lax.psum_scatter(
        moved_rows.astype(jnp.bfloat16), "req", scatter_dimension=0, tiled=True
    ).astype(jnp.float32)
    img_mid = img_float + gate_attn * attn_out
    mlp_in = (layer_norm(img_mid) * (1.0 + scale_mlp) + shift_mlp).astype(jnp.bfloat16)
    raised = jnp.einsum(
        "rnd,df->rnf",
        lax.all_gather(mlp_in, "seq", axis=1, tiled=True),
        fc_in,
        preferred_element_type=jnp.float32,
    )
    hidden = jax.nn.gelu(raised, approximate=True).astype(jnp.bfloat16)
    mlp_terms = jnp.einsum("rnf,fd->rnd", hidden, fc_out, preferred_element_type=jnp.float32)
    mlp_out = lax.psum_scatter(
        mlp_terms.astype(jnp.bfloat16), "seq", scatter_dimension=1, tiled=True
    ).astype(jnp.float32)
    img_out = img_mid + gate_mlp * mlp_out
    final_in = (layer_norm(img_out) * (1.0 + scale_final) + shift_final).astype(jnp.bfloat16)
    own_velocity = jnp.einsum(
        "rnd,dc->rnc", final_in, final_weight, preferred_element_type=jnp.float32
    )
    half_values = latent.shape[2]
    half_index = lax.axis_index("cfg")
    kept_velocity = lax.dynamic_slice_in_dim(own_velocity, half_index * half_values, half_values, 2)
    sent_velocity = lax.dynamic_slice_in_dim(
        own_velocity, (1 - half_index) * half_values, half_values, 2
    )
    other_velocity = from_partner(sent_velocity, "cfg", 0)
    cond_first = half_index == 0
    conditional = jnp.where(cond_first, kept_velocity, other_velocity)
    unconditional = jnp.where(cond_first, other_velocity, kept_velocity)
    guided = unconditional + GUIDANCE * (conditional - unconditional)
    step_size = lax.dynamic_slice_in_dim(upcoming - current, offset, group_size, 0)
    next_latent = latent + step_size[:, None, None] * guided
    squares = jnp.sum(next_latent * next_latent, axis=(1, 2))
    largest = jnp.max(jnp.abs(next_latent), axis=(1, 2))
    square_total = lax.psum(squares, ("cfg", "seq"))
    peak_value = lax.pmax(largest, ("cfg", "seq"))
    latent_norm = jnp.sqrt(square_total / (IMG * PATCHC))
    return (guided, next_latent, latent_norm, peak_value)


def solution(mesh):
    placed = (
        P("cfg", "req", "seq", None),
        P("cfg", "req", "seq", None),
        P("cfg", None),
        P("cfg", None, None),
        P(),
        P("req", "seq", "cfg"),
        P(None, ("req", "seq")),
        P(("req", "seq")),
        P(None, None, "req"),
        P(None, None, "req"),
        P("req", None),
        P(None, "seq"),
        P("seq", None),
        P(),
    )
    return jax.shard_map(
        on_device,
        mesh=mesh,
        in_specs=placed,
        out_specs=(P("req", "seq", "cfg"), P("req", "seq", "cfg"), P("req"), P("req")),
        check_vma=False,
    )
```

profile of v0, /device:TPU:1, one launch (start us, length us, event | category | flops | bytes accessed | tf_op | source)
XLA Modules:
  0.0 808.6 jit_solution(5461950614559532431)
XLA Ops:
  7.2 0.8 divide_subtract_fusion
  8.0 0.3 multiply_cosine_fusion
  8.3 1.2 fusion.18
  9.5 299.6 %all-gather = f32[128,120,16]{1,2,0:T(8,128)S(1)} all-gather(f32[1,120,16]{1,2,0:T(8,128)S(1)} %fusion.18), channel_id=1, replica_groups=mesh['cfg'=2,'req'=8,'seq'=16] {'req','seq'}, dimensions={0}, use_global_device_ids=true | all-gather | bytes 990720 | tf_op jit(solution)/shard_map/all_gather | solution.py:94
  309.1 0.3 copy.26
  309.4 1.6 reshape.180
  311.0 1.1 dynamic-slice_bitcast_fusion
  312.2 0.7 fusion.60
  313.0 0.2 fusion.31
  313.3 0.8 fusion.34
  314.5 19.9 %all_gather.14 = bf16[16,10,1536]{2,1,0:T(8,128)(2,1)S(1)} all-gather(bf16[2,10,1536]{2,1,0:T(8,128)(2,1)S(1)} %fusion.42), channel_id=1, replica_groups=mesh['cfg'=2,'req'=8,'seq'=16] {'req'}, dimensions={0}, use_global_device_ids=true | all-gather | bytes 552960 | tf_op jit(solution)/shard_map/all_gather | solution.py:110
  334.4 13.0 %all_to_all.30 = bf16[16,10,1536]{2,1,0:T(8,128)(2,1)S(1)} all-to-all(bf16[16,10,1536]{2,1,0:T(8,128)(2,1)S(1)} %all_gather.14), channel_id=1, replica_groups=mesh['cfg'=2,'req'=8,'seq'=16] {'seq'}, dimensions={0} | all-to-all | bytes 983040 | tf_op jit(solution)/shard_map/all_to_all | solution.py:118
  347.4 51.1 %all-gather.4.cloned.1.call-done = bf16[16,32,1536]{2,1,0:T(8,128)(2,1)} async-done(((bf16[2,32,1536]{2,1,0:T(8,128)(2,1)}), bf16[16,32,1536]{2,1,0:T(8,128)(2,1)}) %all-gather.4.cloned.1.call-update) | async-done | bytes 1572880 | tf_op jit(solution)/shard_map/all_gather | solution.py:109
  398.5 5.8 all-to-all-start
  404.3 0.2 reduce-scatter.3.cloned.1.call-start
  404.6 0.6 fusion.62
  405.2 0.6 iota_compare_fusion
  406.0 1.7 convolution_convert_fusion.3
  407.8 13.1 %all-to-all-done = bf16[16,32,1536]{2,1,0:T(8,128)(2,1)} async-done(((bf16[16,32,1536]{2,1,0:T(8,128)(2,1)}), bf16[16,32,1536]{2,1,0:T(8,128)(2,1)}, u32[]{:S(2)}, u32[]{:S(2)}) %all-to-all-start) | async-done | bytes 1572896 | tf_op jit(solution)/shard_map/all_to_all | solution.py:117
  420.9 2.5 convolution_convert_fusion.2
  423.5 3.5 fusion.63
  427.1 2.7 fusion.17
  429.8 0.6 fusion.2
  430.4 4.1 copy.58
  434.5 0.5 broadcast.203
  435.0 11.5 %reduce.2 = bf16[512,1536]{1,0:T(8,128)(2,1)S(1)} reduce(bf16[512,1,1536]{2,1,0:T(2,128)(2,1)} %bitcast.126, bf16[]{:T(256)} %broadcast.203), dimensions={1}, to_apply=%bitcast.124.reduce_sub_computation | reduce | bytes 3145730
  446.5 2.1 reshape.184
  448.6 18.4 %all_to_all.31 = bf16[16,2,24576]{2,1,0:T(2,128)(2,1)S(1)} all-to-all(bf16[16,2,24576]{2,1,0:T(2,128)(2,1)} %reshape.184), channel_id=1, replica_groups=mesh['cfg'=2,'req'=8,'seq'=16] {'seq'}, dimensions={0} | all-to-all | bytes 3145728 | tf_op jit(solution)/shard_map/all_to_all | solution.py:156
  466.9 6.3 reshape.185
  473.2 3.4 copy.36
  476.6 0.6 copy-done.5
  477.3 42.2 %reduce-scatter.3.cloned.1.call-done = bf16[2,32,1536]{2,1,0:T(8,128)(2,1)} async-done(((bf16[16,32,1536]{2,1,0:T(8,128)(2,1)}), bf16[2,32,1536]{2,1,0:T(8,128)(2,1)}) %reduce-scatter.3.cloned.1.call-update) | async-done | bytes 196624 | tf_op jit(solution)/shard_map/reduce_scatter | solution.py:159
  519.5 1.1 fusion.35
  520.5 1.1 multiply_reduce_fusion.1
  521.7 1.8 add_convert_fusion.1
  523.5 54.8 %all-gather.6.cloned.1.call-done = bf16[2,512,1536]{2,1,0:T(8,128)(2,1)} async-done(((bf16[2,32,1536]{2,1,0:T(8,128)(2,1)}), bf16[2,512,1536]{2,1,0:T(8,128)(2,1)}) %all-gather.6.cloned.1.call-update) | async-done | bytes 3145744 | tf_op jit(solution)/shard_map/all_gather | solution.py:166
  578.4 7.6 convolution_convert_fusion
  586.0 0.6 copy-done.6
  586.6 78.8 %reduce-scatter.5.cloned.1.call-done = bf16[2,32,1536]{2,1,0:T(8,128)(2,1)} async-done(((bf16[2,512,1536]{2,1,0:T(8,128)(2,1)}), bf16[2,32,1536]{2,1,0:T(8,128)(2,1)}) %reduce-scatter.5.cloned.1.call-update) | async-done | bytes 196624 | tf_op jit(solution)/shard_map/reduce_scatter | solution.py:172
  665.5 1.1 fusion.58
  666.6 1.1 multiply_reduce_fusion
  667.8 1.2 fusion.43
  669.1 2.4 collective-permute-start
  671.6 0.8 collective-permute-done
  672.3 0.7 abs_reduce_fusion
  673.1 65.3 %psum.7 = f32[2]{0:T(128)S(1)} all-reduce(f32[2]{0:T(128)S(1)} %get-tuple-element.41), channel_id=1, replica_groups=mesh['cfg'=2,'req'=8,'seq'=16] {'cfg','seq'}, use_global_device_ids=true, to_apply=%region_13.14 | all-reduce | flops 2 | bytes 16 | tf_op jit(solution)/shard_map/psum | solution.py:195
  738.3 0.5 multiply_sqrt_fusion
  738.8 63.2 %pmax.7 = f32[2]{0:T(128)} all-reduce(f32[2]{0:T(128)S(1)} %get-tuple-element.40), channel_id=1, replica_groups=mesh['cfg'=2,'req'=8,'seq'=16] {'cfg','seq'}, use_global_device_ids=true, to_apply=%region_15.16 | all-reduce | flops 2 | bytes 16 | tf_op jit(solution)/shard_map/pmax | solution.py:196
  (61 shorter events, 1.5 us)
Async XLA Ops:
  7.2 413.7 %copy-start = (bf16[1536,3,192]{0,2,1:T(8,128)(2,1)S(1)}, bf16[1536,3,192]{0,2,1:T(8,128)(2,1)}, u32[]{:S(2)}) copy-start(bf16[1536,3,192]{0,2,1:T(8,128)(2,1)} %param.22) | copy-start | bytes 5308420
  7.2 391.3 %all-gather.4.cloned.1.call-start = ((), (), s32[]{:S(2)}) async-start(), calls=%async_computation.5 | async-start | bytes 1769472 | tf_op jit(solution)/shard_map/all_gather | solution.py:109
  309.4 3.5 copy-start.1
  309.4 4.7 copy-start.4
  347.4 57.1 %copy-start.13 = (s32[1,16]{1,0:T(1,128)S(1)}, s32[1,16]{1,0:T(1,128)}, u32[]{:S(2)}) copy-start(s32[1,16]{1,0:T(1,128)} %param.16) | copy-start | bytes 196
  398.5 22.4 %all-to-all-start = ((bf16[16,32,1536]{2,1,0:T(8,128)(2,1)}), bf16[16,32,1536]{2,1,0:T(8,128)(2,1)}, u32[]{:S(2)}, u32[]{:S(2)}) async-start(bf16[16,32,1536]{2,1,0:T(8,128)(2,1)} %all-gather.4.cloned.1.call-done), calls=%async_computation | async-start | bytes 3145728 | tf_op jit(solution)/shard_map/all_to_all | solution.py:117
  404.3 115.1 %reduce-scatter.3.cloned.1.call-start = ((), (), s32[]{:S(2)}) async-start(), calls=%async_computation.6 | async-start | bytes 1769472 | tf_op jit(solution)/shard_map/reduce_scatter | solution.py:159
  427.1 2.7 copy-start.3
  476.5 0.7 copy-start.5
  476.5 0.7 copy-start.8
  476.5 0.7 copy-start.9
  476.5 101.8 %copy-start.11 = (bf16[384,1536]{1,0:T(8,128)(2,1)S(1)}, bf16[384,1536]{1,0:T(8,128)(2,1)}, u32[]{:S(2)}) copy-start(bf16[384,1536]{1,0:T(8,128)(2,1)} %param.26) | copy-start | bytes 3538948
  476.6 101.8 %all-gather.6.cloned.1.call-start = ((), (), s32[]{:S(2)}) async-start(), calls=%async_computation.7 | async-start | bytes 3342336 | tf_op jit(solution)/shard_map/all_gather | solution.py:166
  523.5 142.0 %reduce-scatter.5.cloned.1.call-start = ((), (), s32[]{:S(2)}) async-start(), calls=%async_computation.8 | async-start | bytes 3342336 | tf_op jit(solution)/shard_map/reduce_scatter | solution.py:172
  585.9 0.7 copy-start.6
  585.9 0.7 copy-start.7
  585.9 79.6 %copy-start.2 = (bf16[2,32,1536]{2,1,0:T(8,128)(2,1)S(1)}, bf16[2,32,1536]{2,1,0:T(8,128)(2,1)}, u32[]{:S(2)}) copy-start(bf16[2,32,1536]{2,1,0:T(8,128)(2,1)} %reduce-scatter.3.cloned.1.call-done) | copy-start | bytes 589828
  585.9 81.9 %copy-start.12 = (bf16[1536,64]{0,1:T(8,128)(2,1)S(1)}, bf16[1536,64]{0,1:T(8,128)(2,1)}, u32[]{:S(2)}) copy-start(bf16[1536,64]{0,1:T(8,128)(2,1)} %param.27) | copy-start | bytes 589828
  585.9 86.4 %copy-start.10 = (f32[2,32,32]{2,1,0:T(8,128)S(1)}, f32[2,32,32]{2,1,0:T(8,128)}, u32[]{:S(2)}) copy-start(f32[2,32,32]{2,1,0:T(8,128)} %param.19) | copy-start | bytes 24580
  669.1 3.3 collective-permute-start
Sparse Core Ops, SparseCore 0:
  314.2 84.2 all-gather.3
  476.7 42.7 reduce-scatter.2
  523.6 54.7 all-gather.5
  586.1 79.3 reduce-scatter.4
where the time goes:
time: 809 us
  blocking collectives  479 us (59%)
  waiting for transfers between devices  241 us (30%)
  other arithmetic  23.5 us (3%)
  local copies, waits for them, and re-layouts  21.2 us (3%)
  matrix products  21.1 us (3%)
  between operations  14 us (2%)
  starting transfers between devices  8.55 us (1%)
    all_gather x1, blocking collectives, on_device(): every_mod = lax.all_gather(columns, ('req', 'seq'), axis=1, tiled=True)  300 us
    reduce_scatter x1, waiting for transfers between devices, on_device(): lax.psum_scatter(mlp_terms.astype(jnp.bfloat16), 'seq', scatter_dimension...  78.8 us
    psum x1, blocking collectives, on_device(): square_total = lax.psum(squares, ('cfg', 'seq'))  65.3 us
    pmax x1, blocking collectives, on_device(): peak_value = lax.pmax(largest, ('cfg', 'seq'))  63.2 us
    all_gather x1, waiting for transfers between devices, on_device(): lax.all_gather(mlp_in, 'seq', axis=1, tiled=True)  54.8 us
    all_gather x1, waiting for transfers between devices, on_device(): lax.all_gather(img_in, 'req', axis=0, tiled=True)  51.1 us
    reduce_scatter x1, waiting for transfers between devices, on_device(): lax.psum_scatter(moved_rows.astype(jnp.bfloat16), 'req', scatter_dimensio...  42.2 us
    all_gather x1, blocking collectives, on_device(): lax.all_gather(txt_in, 'req', axis=0, tiled=True)  19.9 us
  transfers between devices with their start and end apart: 6, of which 6 were waited for; matrix products, arithmetic and copies ran while one was open for 0% of the time, Pallas kernels for 0%

commit v1 on v0

v1 whole, which is shorter than its diff:
```python
import math

import jax
import jax.numpy as jnp
from jax import lax
from jax.sharding import PartitionSpec as P

D = 1536
HD = 64
PATCHC = 64
IMG = 512
STEPS = 28


SIGMA_SHIFT = 3.0
GUIDANCE = 5.0
EPSILON = 1e-06
MASKED_SCORE = -1e30


def xor_pairs(axis, distance):
    return [(source, source ^ distance) for source in range(lax.axis_size(axis))]


def shifted(fraction):
    return SIGMA_SHIFT * fraction / (1.0 + (SIGMA_SHIFT - 1.0) * fraction)


def plan(timestep):
    position = timestep.astype(jnp.float32)
    return (shifted(1.0 - position / STEPS), shifted(1.0 - (position + 1.0) / STEPS))


def time_features(sigma):
    half_width = D // 2
    frequency = jnp.exp(-math.log(10000.0) * jnp.arange(half_width, dtype=jnp.float32) / half_width)
    angles = (1000.0 * sigma)[:, None] * frequency[None, :]
    return jnp.concatenate([jnp.cos(angles), jnp.sin(angles)], axis=1)


def layer_norm(values):
    average = jnp.mean(values, axis=-1, keepdims=True)
    centred = values - average
    spread = jnp.mean(centred * centred, axis=-1, keepdims=True)
    return centred * lax.rsqrt(spread + EPSILON)


def gather_by_a2a(value, axis):
    count = lax.axis_size(axis)
    copies = jnp.broadcast_to(value[None], (count,) + value.shape)
    return lax.all_to_all(copies, axis, 0, 0, tiled=True)


def attention(queries, key_rows, value_rows, live_keys):
    scale_factor = HD ** (-0.5)
    scores = (
        jnp.einsum("qhd,khd->hqk", queries, key_rows, preferred_element_type=jnp.float32)
        * scale_factor
    )
    scores = jnp.where(live_keys[None, None, :], scores, MASKED_SCORE)
    highest = jnp.max(scores, axis=-1, keepdims=True)
    exp_scores = jnp.exp(scores - highest)
    weights = (exp_scores / jnp.sum(exp_scores, axis=-1, keepdims=True)).astype(jnp.bfloat16)
    mixture = jnp.einsum("hqk,khd->qhd", weights, value_rows, preferred_element_type=jnp.float32)
    return mixture.astype(jnp.bfloat16)


def on_device(
    img_hidden,
    txt_hidden,
    text_len,
    pooled,
    timestep,
    latent,
    mod_weight,
    mod_bias,
    img_qkv,
    txt_kv,
    out_weight,
    fc_in,
    fc_out,
    final_weight,
):
    group_size = img_hidden.shape[1]
    req_count = lax.axis_size("req")
    seq_count = lax.axis_size("seq")
    current, upcoming = plan(timestep)
    activated = jax.nn.silu(pooled[0] + time_features(current)).astype(jnp.bfloat16)
    columns = jnp.dot(activated, mod_weight, preferred_element_type=jnp.float32) + mod_bias
    block_width = columns.shape[1]
    mine = lax.all_to_all(
        columns.reshape(req_count, group_size, block_width), "req", 0, 0, tiled=True
    )
    every = gather_by_a2a(mine, "seq")
    every = every.transpose(2, 1, 0, 3).reshape(group_size, req_count * seq_count * block_width)
    modulation = every.reshape(group_size, 10, 1, D)
    shift_attn, scale_attn, gate_attn = (modulation[:, 0], modulation[:, 1], modulation[:, 2])
    shift_mlp, scale_mlp, gate_mlp = (modulation[:, 3], modulation[:, 4], modulation[:, 5])
    shift_text, scale_text = (modulation[:, 6], modulation[:, 7])
    scale_final, shift_final = (modulation[:, 8], modulation[:, 9])
    img_float = img_hidden[0].astype(jnp.float32)
    img_in = (layer_norm(img_float) * (1.0 + scale_attn) + shift_attn).astype(jnp.bfloat16)
    txt_in = (
        layer_norm(txt_hidden[0].astype(jnp.float32)) * (1.0 + scale_text) + shift_text
    ).astype(jnp.bfloat16)
    row_count = img_in.shape[1]
    text_block = txt_in.shape[1]
    both = gather_by_a2a(jnp.concatenate([img_in, txt_in], axis=1), "req")
    both = both.reshape(req_count * group_size, row_count + text_block, D)
    head_width = img_qkv.shape[2]
    local_heads = head_width // HD
    qkv_columns = img_qkv.reshape(D, 3 * head_width)
    kv_columns = txt_kv.reshape(D, 2 * head_width)
    proj_img = jnp.einsum(
        "rnd,dc->rnc", both[:, :row_count], qkv_columns, preferred_element_type=jnp.float32
    ).astype(jnp.bfloat16)
    proj_txt = jnp.einsum(
        "rnd,dc->rnc", both[:, row_count:], kv_columns, preferred_element_type=jnp.float32
    ).astype(jnp.bfloat16)
    request_count = proj_img.shape[0]
    img_size = row_count * 3 * head_width
    packed = jnp.concatenate(
        [proj_img.reshape(request_count, img_size), proj_txt.reshape(request_count, -1)], axis=1
    )
    own = lax.all_to_all(packed, "seq", 0, 0, tiled=True)
    image_rows = seq_count * row_count
    text_rows = seq_count * text_block
    own_img = own[:, :img_size].reshape(image_rows, 3 * head_width)
    own_txt = own[:, img_size:].reshape(text_rows, 2 * head_width)
    queries = own_img[:, :head_width]
    key_rows = jnp.concatenate([own_img[:, head_width : 2 * head_width], own_txt[:, :head_width]], 0)
    value_rows = jnp.concatenate([own_img[:, 2 * head_width :], own_txt[:, head_width:]], 0)
    text_count = lax.dynamic_index_in_dim(text_len[0], lax.axis_index("seq"), 0, False)
    total_keys = image_rows + text_rows
    live_keys = jnp.arange(total_keys, dtype=jnp.int32) < image_rows + text_count
    attended = attention(
        queries.reshape(image_rows, local_heads, HD),
        key_rows.reshape(total_keys, local_heads, HD),
        value_rows.reshape(total_keys, local_heads, HD),
        live_keys,
    ).reshape(seq_count, row_count, head_width)
    attended_rows = lax.all_to_all(attended, "seq", 0, 0, tiled=True)
    partial = jnp.einsum(
        "rnk,kd->rnd", attended_rows, out_weight, preferred_element_type=jnp.float32
    ).astype(jnp.bfloat16)
    head_terms = lax.all_to_all(
        partial.reshape(req_count, group_size, row_count, D), "req", 0, 0, tiled=True
    )
    attn_out = jnp.sum(head_terms.astype(jnp.float32), axis=0)
    img_mid = img_float + gate_attn * attn_out
    mlp_in = (layer_norm(img_mid) * (1.0 + scale_mlp) + shift_mlp).astype(jnp.bfloat16)
    all_rows = gather_by_a2a(mlp_in, "seq")
    raised = jnp.einsum("srnd,df->srnf", all_rows, fc_in, preferred_element_type=jnp.float32)
    hidden = jax.nn.gelu(raised, approximate=True).astype(jnp.bfloat16)
    mlp_terms = jnp.einsum(
        "srnf,fd->srnd", hidden, fc_out, preferred_element_type=jnp.float32
    ).astype(jnp.bfloat16)
    block_terms = lax.all_to_all(mlp_terms, "seq", 0, 0, tiled=True)
    mlp_out = jnp.sum(block_terms.astype(jnp.float32), axis=0)
    img_out = img_mid + gate_mlp * mlp_out
    final_in = (layer_norm(img_out) * (1.0 + scale_final) + shift_final).astype(jnp.bfloat16)
    own_velocity = jnp.einsum(
        "rnd,dc->rnc", final_in, final_weight, preferred_element_type=jnp.float32
    )
    half_values = latent.shape[2]
    half_index = lax.axis_index("cfg")
    kept_velocity = lax.dynamic_slice_in_dim(own_velocity, half_index * half_values, half_values, 2)
    sent_velocity = lax.dynamic_slice_in_dim(
        own_velocity, (1 - half_index) * half_values, half_values, 2
    )
    other_velocity = lax.ppermute(sent_velocity, "cfg", xor_pairs("cfg", 1))
    cond_first = half_index == 0
    conditional = jnp.where(cond_first, kept_velocity, other_velocity)
    unconditional = jnp.where(cond_first, other_velocity, kept_velocity)
    guided = unconditional + GUIDANCE * (conditional - unconditional)
    offset = lax.axis_index("req") * group_size
    step_size = lax.dynamic_slice_in_dim(upcoming - current, offset, group_size, 0)
    next_latent = latent + step_size[:, None, None] * guided
    squares = jnp.sum(next_latent * next_latent, axis=(1, 2))
    largest = jnp.max(jnp.abs(next_latent), axis=(1, 2))
    for axis, distance in (("seq", 1), ("seq", 2), ("seq", 4), ("seq", 8), ("cfg", 1)):
        if distance >= lax.axis_size(axis):
            continue
        stats = lax.ppermute(jnp.stack([squares, largest]), axis, xor_pairs(axis, distance))
        squares = squares + stats[0]
        largest = jnp.maximum(largest, stats[1])
    latent_norm = jnp.sqrt(squares / (IMG * PATCHC))
    return (guided, next_latent, latent_norm, largest)


def solution(mesh):
    placed = (
        P("cfg", "req", "seq", None),
        P("cfg", "req", "seq", None),
        P("cfg", None),
        P("cfg", None, None),
        P(),
        P("req", "seq", "cfg"),
        P(None, ("req", "seq")),
        P(("req", "seq")),
        P(None, None, "req"),
        P(None, None, "req"),
        P("req", None),
        P(None, "seq"),
        P("seq", None),
        P(),
    )
    return jax.shard_map(
        on_device,
        mesh=mesh,
        in_specs=placed,
        out_specs=(P("req", "seq", "cfg"), P("req", "seq", "cfg"), P("req"), P("req")),
        check_vma=False,
    )
```

time: 809 us -> 299 us (0.37)
  blocking collectives: 479 us -> 100 us
  waiting for transfers between devices: 241 us -> 104 us
  starting transfers between devices: 8.55 us -> 44.1 us
  between operations: 14 us -> 1.15 us
  other arithmetic: 23.5 us -> 15.2 us
    all_gather x2 -> x0, blocking collectives: 319 us -> none  [the longest x1 300 us: on_device(): every_mod = lax.all_gather(columns, ('req', 'seq'), axis=1, tiled=True)]
    reduce_scatter x2 -> x0, waiting for transfers between devices: 121 us -> none  [the longest x1 78.8 us: on_device(): lax.psum_scatter(mlp_terms.astype(jnp.bfloat16), 'seq', scatter_dimension...]
    all_gather x2 -> x0, waiting for transfers between devices: 106 us -> none  [the longest x1 54.8 us: on_device(): lax.all_gather(mlp_in, 'seq', axis=1, tiled=True)]
    all_to_all x1 -> x5, waiting for transfers between devices: 13.1 us -> 90.4 us  [the longest x1 36.4 us: on_device(): lax.all_to_all(partial.reshape(req_count, group_size, row_count, D), 'req...]
    all_to_all x2 -> x3, blocking collectives: 31.3 us -> 100 us  [the longest x2 90 us: gather_by_a2a(): return lax.all_to_all(copies, axis, 0, 0, tiled=True)]
    psum x1 -> x0, blocking collectives: 65.3 us -> none  [on_device(): square_total = lax.psum(squares, ('cfg', 'seq'))]
    pmax x1 -> x0, blocking collectives: 63.2 us -> none  [on_device(): peak_value = lax.pmax(largest, ('cfg', 'seq'))]
    all_to_all x1 -> x5, starting transfers between devices: 5.82 us -> 30.3 us  [the longest x1 9 us: on_device(): lax.all_to_all(columns.reshape(req_count, group_size, block_width), 'req'...]
  transfers between devices with their start and end apart: 6 -> 11, of which waited for: 6 -> 11; matrix products, arithmetic and copies ran while one was open for 0% -> 2% of each run, Pallas kernels for 0% -> 0%
where the time goes in v1:
time: 299 us; the launch traced here: 298 us
  waiting for transfers between devices  104 us (35%)
  blocking collectives  100 us (33%)
  starting transfers between devices  44.1 us (15%)
  matrix products  19.8 us (7%)
  other arithmetic  15.2 us (5%)
  local copies, waits for them, and re-layouts  13.5 us (5%)
    all_to_all x2, blocking collectives, gather_by_a2a(): return lax.all_to_all(copies, axis, 0, 0, tiled=True)  90 us
    all_to_all x1, waiting for transfers between devices, on_device(): lax.all_to_all(partial.reshape(req_count, group_size, row_count, D), 'req...  36.4 us
    all_to_all x1, waiting for transfers between devices, on_device(): block_terms = lax.all_to_all(mlp_terms, 'seq', 0, 0, tiled=True)  35.7 us
    ppermute x5, waiting for transfers between devices, on_device(): lax.ppermute(jnp.stack([squares, largest]), axis, xor_pairs(axis, distance))  12.9 us
    all_to_all x1, blocking collectives, on_device(): attended_rows = lax.all_to_all(attended, 'seq', 0, 0, tiled=True)  10.1 us
    all_to_all x1, waiting for transfers between devices, on_device(): own = lax.all_to_all(packed, 'seq', 0, 0, tiled=True)  9.07 us
    all_to_all x1, starting transfers between devices, on_device(): lax.all_to_all(columns.reshape(req_count, group_size, block_width), 'req'...  9 us
    dot_general x1, matrix products, on_device(): jnp.einsum('srnf,fd->srnd', hidden, fc_out, preferred_element_type=jnp.fl...  7.87 us
  transfers between devices with their start and end apart: 11, of which 11 were waited for; matrix products, arithmetic and copies ran while one was open for 2% of the time, Pallas kernels for 0%

profile of v1, /device:TPU:1, one launch (start us, length us, event | category | flops | bytes accessed | tf_op | source)
XLA Modules:
  0.0 297.9 jit_solution(11415721194773044029)
XLA Ops:
  0.7 0.8 divide_subtract_fusion
  1.8 1.8 convolution_add_fusion
  3.6 9.0 %all-to-all-start = ((f32[8,2,120]{2,1,0:T(2,128)}), f32[8,2,120]{2,1,0:T(2,128)S(1)}, u32[]{:S(2)}, u32[]{:S(2)}) async-start(f32[8,2,120]{2,1,0:T(2,128)} %bitcast.2), calls=%async_computation | async-start | bytes 16384 | tf_op jit(solution)/shard_map/all_to_all | solution.py:91
  12.6 1.0 convert_reduce_fusion.3
  13.5 1.0 fusion.56
  14.6 1.0 convert_reduce_fusion.2
  15.7 1.1 fusion.37
  16.8 2.4 all-to-all-done
  19.2 0.6 broadcast_in_dim.16
  19.8 6.8 %all-to-all-start.1 = ((f32[16,8,2,120]{3,1,2,0:T(8,128)}), f32[16,8,2,120]{3,1,2,0:T(8,128)S(1)}, u32[]{:S(2)}, u32[]{:S(2)}) async-start(f32[16,8,2,120]{3,1,2,0:T(8,128)} %broadcast_in_dim.16), calls=%async_computation.1 | async-start | bytes 262144 | tf_op jit(solution)/shard_map/all_to_all | solution.py:51
  26.6 6.8 %all-to-all-done.1 = f32[16,8,2,120]{3,1,2,0:T(8,128)S(1)} async-done(((f32[16,8,2,120]{3,1,2,0:T(8,128)}), f32[16,8,2,120]{3,1,2,0:T(8,128)S(1)}, u32[]{:S(2)}, u32[]{:S(2)}) %all-to-all-start.1) | async-done | bytes 122912 | tf_op jit(solution)/shard_map/all_to_all | solution.py:51
  33.6 0.7 slice_add_fusion
  35.1 1.1 broadcast_in_dim.17
  36.1 51.1 %all_to_all.47 = bf16[8,2,42,1536]{3,1,2,0:T(2,128)(2,1)S(1)} all-to-all(bf16[8,2,42,1536]{3,1,2,0:T(2,128)(2,1)S(1)} %broadcast_in_dim.17), channel_id=1, replica_groups=mesh['cfg'=2,'req'=8,'seq'=16] {'req'}, dimensions={0} | all-to-all | bytes 4128768 | tf_op jit(solution)/shard_map/all_to_all | solution.py:51
  87.7 0.8 copy-done.11
  88.5 0.6 convolution_convert_fusion.2
  89.1 1.4 fusion.16
  90.6 0.8 reshape.179
  91.9 1.2 reduce.2
  93.1 1.1 reshape.195
  94.2 4.3 %all-to-all-start.3 = ((bf16[16,2,11136]{2,1,0:T(2,128)(2,1)}), bf16[16,2,11136]{2,1,0:T(2,128)(2,1)}, u32[]{:S(2)}, u32[]{:S(2)}) async-start(bf16[16,2,11136]{2,1,0:T(2,128)(2,1)} %reshape.195), calls=%async_computation.3 | async-start | bytes 1425408 | tf_op jit(solution)/shard_map/all_to_all | solution.py:125
  98.5 0.6 fusion.75
  99.0 0.6 iota_compare_fusion
  99.7 9.1 %all-to-all-done.3 = bf16[16,2,11136]{2,1,0:T(2,128)(2,1)} async-done(((bf16[16,2,11136]{2,1,0:T(2,128)(2,1)}), bf16[16,2,11136]{2,1,0:T(2,128)(2,1)}, u32[]{:S(2)}, u32[]{:S(2)}) %all-to-all-start.3) | async-done | bytes 712736 | tf_op jit(solution)/shard_map/all_to_all | solution.py:125
  108.8 4.2 %reshape.196 = bf16[16,1,22272]{2,1,0:T(2,128)(2,1)S(1)} reshape(bf16[16,2,11136]{2,1,0:T(2,128)(2,1)} %all-to-all-done.3) | data formatting | bytes 1425408
  113.4 0.8 reshape.182
  114.9 3.5 %fusion.76 = (f32[3,512]{1,0:T(4,128)S(1)}, f32[3,512,672]{1,2,0:T(8,128)}) fusion(pred[672]{0:T(1024)(128)(4,1)S(1)} %iota_compare_fusion, bf16[512,3,64]{0,2,1:T(8,128)(2,1)S(1)} %bitcast.186, bf16[672,3,64]{0,2,1:T(8,128)(2,1)S(1)} %bitcast.185), kind=kOutput, calls=%fused_computation.156 | convolution fusion | flops 136250016 | bytes 4590240 | tf_op jit(solution)/shard_map/sub | solution.py:62
  118.4 2.7 fusion.22
  121.7 10.1 %all_to_all.48 = bf16[16,32,192]{2,1,0:T(8,128)(2,1)S(1)} all-to-all(bf16[16,32,192]{2,1,0:T(8,128)(2,1)S(1)} %reshape.187), channel_id=1, replica_groups=mesh['cfg'=2,'req'=8,'seq'=16] {'seq'}, dimensions={0} | all-to-all | bytes 393216 | tf_op jit(solution)/shard_map/all_to_all | solution.py:142
  131.8 1.7 convolution_convert_fusion.1
  133.5 5.6 %all-to-all-start.5 = ((bf16[8,2,32,1536]{3,2,1,0:T(8,128)(2,1)}), bf16[8,2,32,1536]{3,2,1,0:T(8,128)(2,1)}, u32[]{:S(2)}, u32[]{:S(2)}) async-start(bf16[8,2,32,1536]{3,2,1,0:T(8,128)(2,1)} %bitcast.17), calls=%async_computation.5 | async-start | bytes 3145728 | tf_op jit(solution)/shard_map/all_to_all | solution.py:146
  139.2 36.4 %all-to-all-done.5 = bf16[8,2,32,1536]{3,2,1,0:T(8,128)(2,1)} async-done(((bf16[8,2,32,1536]{3,2,1,0:T(8,128)(2,1)}), bf16[8,2,32,1536]{3,2,1,0:T(8,128)(2,1)}, u32[]{:S(2)}, u32[]{:S(2)}) %all-to-all-start.5) | async-done | bytes 1572896 | tf_op jit(solution)/shard_map/all_to_all | solution.py:146
  175.7 1.7 convert_reduce_fusion.1
  178.2 38.9 %all_to_all.49 = bf16[16,2,32,1536]{3,2,1,0:T(8,128)(2,1)} all-to-all(bf16[16,2,32,1536]{3,2,1,0:T(8,128)(2,1)S(1)} %broadcast_in_dim.25), channel_id=1, replica_groups=mesh['cfg'=2,'req'=8,'seq'=16] {'seq'}, dimensions={0} | all-to-all | bytes 6291456 | tf_op jit(solution)/shard_map/all_to_all | solution.py:51
  217.1 7.9 %convolution_convert_fusion = bf16[16,2,32,1536]{3,2,1,0:T(8,128)(2,1)} fusion(bf16[384,1536]{1,0:T(8,128)(2,1)} %param.26, bf16[16,2,32,1536]{3,2,1,0:T(8,128)(2,1)} %all_to_all.49, bf16[1536,384]{1,0:T(8,128)(2,1)} %param.25), kind=kOutput, calls=%fused_computation.5 | convolution fusion | flops 2421030912 | bytes 8650752 | tf_op jit(solution)/shard_map/srnf,fd->srnd/dot_general | solution.py:155
  225.0 4.6 %all-to-all-start.7 = ((bf16[16,2,32,1536]{3,2,1,0:T(8,128)(2,1)}), bf16[16,2,32,1536]{3,2,1,0:T(8,128)(2,1)}, u32[]{:S(2)}, u32[]{:S(2)}) async-start(bf16[16,2,32,1536]{3,2,1,0:T(8,128)(2,1)} %convolution_convert_fusion), calls=%async_computation.7 | async-start | bytes 6291456 | tf_op jit(solution)/shard_map/all_to_all | solution.py:158
  229.7 35.7 %all-to-all-done.7 = bf16[16,2,32,1536]{3,2,1,0:T(8,128)(2,1)} async-done(((bf16[16,2,32,1536]{3,2,1,0:T(8,128)(2,1)}), bf16[16,2,32,1536]{3,2,1,0:T(8,128)(2,1)}, u32[]{:S(2)}, u32[]{:S(2)}) %all-to-all-start.7) | async-done | bytes 3145760 | tf_op jit(solution)/shard_map/all_to_all | solution.py:158
  265.4 2.4 convert_reduce_fusion
  269.0 7.8 %collective-permute-start = (f32[2,32,32]{2,1,0:T(8,128)S(1)}, f32[2,32,32]{2,1,0:T(8,128)S(1)}, u32[]{:S(2)}, u32[]{:S(2)}) collective-permute-start(f32[2,32,32]{2,1,0:T(8,128)S(1)} %constant_dynamic-slice_fusion), channel_id=1, source_target_pairs={{0,128},{128,0},{1,129},{129,1},{2,130},{130,2},{3,131},{131,3},{4... | collective-permute-start | bytes 24584 | tf_op jit(solution)/shard_map/ppermute | solution.py:171
  276.9 0.8 collective-permute-done
  277.7 0.7 abs_reduce_fusion
  278.5 2.4 collective-permute-done.1
  281.1 3.9 %collective-permute-done.2 = f32[2,2]{1,0:T(2,128)S(1)} collective-permute-done((f32[2,2]{1,0:T(2,128)S(1)}, f32[2,2]{1,0:T(2,128)S(1)}, u32[]{:S(2)}, u32[]{:S(2)}) %collective-permute-start.2) | collective-permute-done | bytes 48 | tf_op jit(solution)/shard_map/ppermute | solution.py:184
  285.1 2.4 collective-permute-done.3
  287.5 0.7 collective-permute-start.4
  288.2 3.3 %collective-permute-done.4 = f32[2,2]{1,0:T(2,128)S(1)} collective-permute-done((f32[2,2]{1,0:T(2,128)S(1)}, f32[2,2]{1,0:T(2,128)S(1)}, u32[]{:S(2)}, u32[]{:S(2)}) %collective-permute-start.4) | collective-permute-done | bytes 48 | tf_op jit(solution)/shard_map/ppermute | solution.py:184
  291.6 5.0 %collective-permute-start.5 = (f32[2,2]{1,0:T(2,128)S(1)}, f32[2,2]{1,0:T(2,128)S(1)}, u32[]{:S(2)}, u32[]{:S(2)}) collective-permute-start(f32[2,2]{1,0:T(2,128)S(1)} %pad_maximum_fusion.7), channel_id=1, source_target_pairs={{0,128},{128,0},{1,129},{129,1},{2,130},{130,2},{3,131},{131,3},{4... | collective-permute-start | bytes 56 | tf_op jit(solution)/shard_map/ppermute | solution.py:184
  296.6 0.8 collective-permute-done.5
  (89 shorter events, 7.0 us)
Async XLA Ops:
  0.6 88.5 %copy-start = (bf16[1536,3,192]{0,2,1:T(8,128)(2,1)S(1)}, bf16[1536,3,192]{0,2,1:T(8,128)(2,1)}, u32[]{:S(2)}) copy-start(bf16[1536,3,192]{0,2,1:T(8,128)(2,1)} %param.22) | copy-start | bytes 5308420
  0.6 33.7 %copy-start.3 = (bf16[1,2,10,1536]{3,1,2,0:T(2,128)(2,1)S(1)}, bf16[1,2,10,1536]{3,1,2,0:T(2,128)(2,1)}, u32[]{:S(2)}) copy-start(bf16[1,2,10,1536]{3,1,2,0:T(2,128)(2,1)} %param.15) | copy-start | bytes 184324
  0.7 33.9 %copy-start.1 = (bf16[1,2,32,1536]{3,2,1,0:T(8,128)(2,1)S(1)}, bf16[1,2,32,1536]{3,2,1,0:T(8,128)(2,1)}, u32[]{:S(2)}) copy-start(bf16[1,2,32,1536]{3,2,1,0:T(8,128)(2,1)} %param.14) | copy-start | bytes 589828
  3.6 15.6 %all-to-all-start = ((f32[8,2,120]{2,1,0:T(2,128)}), f32[8,2,120]{2,1,0:T(2,128)S(1)}, u32[]{:S(2)}, u32[]{:S(2)}) async-start(f32[8,2,120]{2,1,0:T(2,128)} %bitcast.2), calls=%async_computation | async-start | bytes 16384 | tf_op jit(solution)/shard_map/all_to_all | solution.py:91
  19.8 13.6 %all-to-all-start.1 = ((f32[16,8,2,120]{3,1,2,0:T(8,128)}), f32[16,8,2,120]{3,1,2,0:T(8,128)S(1)}, u32[]{:S(2)}, u32[]{:S(2)}) async-start(f32[16,8,2,120]{3,1,2,0:T(8,128)} %broadcast_in_dim.16), calls=%async_computation.1 | async-start | bytes 262144 | tf_op jit(solution)/shard_map/all_to_all | solution.py:51
  87.2 1.3 copy-start.11
  93.1 5.4 %copy-start.12 = (s32[1,16]{1,0:T(1,128)S(1)}, s32[1,16]{1,0:T(1,128)}, u32[]{:S(2)}) copy-start(s32[1,16]{1,0:T(1,128)} %param.16) | copy-start | bytes 196
  94.2 14.6 %all-to-all-start.3 = ((bf16[16,2,11136]{2,1,0:T(2,128)(2,1)}), bf16[16,2,11136]{2,1,0:T(2,128)(2,1)}, u32[]{:S(2)}, u32[]{:S(2)}) async-start(bf16[16,2,11136]{2,1,0:T(2,128)(2,1)} %reshape.195), calls=%async_computation.3 | async-start | bytes 1425408 | tf_op jit(solution)/shard_map/all_to_all | solution.py:125
  121.0 10.8 %copy-start.2 = (bf16[192,1536]{1,0:T(8,128)(2,1)S(1)}, bf16[192,1536]{1,0:T(8,128)(2,1)}, u32[]{:S(2)}) copy-start(bf16[192,1536]{1,0:T(8,128)(2,1)} %param.24) | copy-start | bytes 1769476
  133.5 5.6 %copy-start.5 = (f32[2,1,1,1536]{3,1,0,2:T(1,128)S(1)}, f32[2,1,1,1536]{3,1,0,2:T(1,128)}, u32[]{:S(2)}) copy-start(f32[2,1,1,1536]{3,1,0,2:T(1,128)} %get-tuple-element.24) | copy-start | bytes 36868
  133.5 5.7 %copy-start.8 = (f32[2,1,1,1536]{3,1,0,2:T(1,128)S(1)}, f32[2,1,1,1536]{3,1,0,2:T(1,128)}, u32[]{:S(2)}) copy-start(f32[2,1,1,1536]{3,1,0,2:T(1,128)} %get-tuple-element.17) | copy-start | bytes 36868
  133.5 5.7 %copy-start.9 = (f32[2,1,1,1536]{3,1,0,2:T(1,128)S(1)}, f32[2,1,1,1536]{3,1,0,2:T(1,128)}, u32[]{:S(2)}) copy-start(f32[2,1,1,1536]{3,1,0,2:T(1,128)} %get-tuple-element.18) | copy-start | bytes 36868
  133.5 42.1 %all-to-all-start.5 = ((bf16[8,2,32,1536]{3,2,1,0:T(8,128)(2,1)}), bf16[8,2,32,1536]{3,2,1,0:T(8,128)(2,1)}, u32[]{:S(2)}, u32[]{:S(2)}) async-start(bf16[8,2,32,1536]{3,2,1,0:T(8,128)(2,1)} %bitcast.17), calls=%async_computation.5 | async-start | bytes 3145728 | tf_op jit(solution)/shard_map/all_to_all | solution.py:146
  225.0 4.7 %copy-start.6 = (f32[2,1,1,1536]{3,1,0,2:T(1,128)S(1)}, f32[2,1,1,1536]{3,1,0,2:T(1,128)}, u32[]{:S(2)}) copy-start(f32[2,1,1,1536]{3,1,0,2:T(1,128)} %get-tuple-element.15) | copy-start | bytes 36868
  225.0 4.7 %copy-start.7 = (f32[2,1,1,1536]{3,1,0,2:T(1,128)S(1)}, f32[2,1,1,1536]{3,1,0,2:T(1,128)}, u32[]{:S(2)}) copy-start(f32[2,1,1,1536]{3,1,0,2:T(1,128)} %get-tuple-element.16) | copy-start | bytes 36868
  225.0 40.4 %all-to-all-start.7 = ((bf16[16,2,32,1536]{3,2,1,0:T(8,128)(2,1)}), bf16[16,2,32,1536]{3,2,1,0:T(8,128)(2,1)}, u32[]{:S(2)}, u32[]{:S(2)}) async-start(bf16[16,2,32,1536]{3,2,1,0:T(8,128)(2,1)} %convolution_convert_fusion), calls=%async_computation.7 | async-start | bytes 6291456 | tf_op jit(solution)/shard_map/all_to_all | solution.py:158
  267.8 0.9 copy-start.4
  267.8 10.0 %copy-start.10 = (f32[2,32,32]{2,1,0:T(8,128)S(1)}, f32[2,32,32]{2,1,0:T(8,128)}, u32[]{:S(2)}) copy-start(f32[2,32,32]{2,1,0:T(8,128)} %param.19) | copy-start | bytes 24580
  269.0 8.7 %collective-permute-start = (f32[2,32,32]{2,1,0:T(8,128)S(1)}, f32[2,32,32]{2,1,0:T(8,128)S(1)}, u32[]{:S(2)}, u32[]{:S(2)}) collective-permute-start(f32[2,32,32]{2,1,0:T(8,128)S(1)} %constant_dynamic-slice_fusion), channel_id=1, source_target_pairs={{0,128},{128,0},{1,129},{129,1},{2,130},{130,2},{3,131},{131,3},{4... | collective-permute-start | bytes 24584 | tf_op jit(solution)/shard_map/ppermute | solution.py:171
  278.5 2.5 collective-permute-start.1
  281.0 4.0 %collective-permute-start.2 = (f32[2,2]{1,0:T(2,128)S(1)}, f32[2,2]{1,0:T(2,128)S(1)}, u32[]{:S(2)}, u32[]{:S(2)}) collective-permute-start(f32[2,2]{1,0:T(2,128)S(1)} %pad_maximum_fusion.4), channel_id=1, source_target_pairs={{0,2},{1,3},{2,0},{3,1},{4,6},{5,7},{6,4},{7,5},{8,10},{9,11},{10,... | collective-permute-start | bytes 56 | tf_op jit(solution)/shard_map/ppermute | solution.py:184
  285.0 2.5 collective-permute-start.3
  287.5 4.0 %collective-permute-start.4 = (f32[2,2]{1,0:T(2,128)S(1)}, f32[2,2]{1,0:T(2,128)S(1)}, u32[]{:S(2)}, u32[]{:S(2)}) collective-permute-start(f32[2,2]{1,0:T(2,128)S(1)} %pad_maximum_fusion.6), channel_id=1, source_target_pairs={{0,8},{1,9},{2,10},{3,11},{4,12},{5,13},{6,14},{7,15},{8,0},{9,1},... | collective-permute-start | bytes 56 | tf_op jit(solution)/shard_map/ppermute | solution.py:184
  291.6 5.9 %collective-permute-start.5 = (f32[2,2]{1,0:T(2,128)S(1)}, f32[2,2]{1,0:T(2,128)S(1)}, u32[]{:S(2)}, u32[]{:S(2)}) collective-permute-start(f32[2,2]{1,0:T(2,128)S(1)} %pad_maximum_fusion.7), channel_id=1, source_target_pairs={{0,128},{128,0},{1,129},{129,1},{2,130},{130,2},{3,131},{131,3},{4... | collective-permute-start | bytes 56 | tf_op jit(solution)/shard_map/ppermute | solution.py:184

commit v2 on v1

--- a/solution.py
+++ b/solution.py
@@ -84,6 +84,28 @@
     group_size = img_hidden.shape[1]
     req_count = lax.axis_size("req")
     seq_count = lax.axis_size("seq")
+    half_index = lax.axis_index("cfg")
+    cond_first = half_index == 0
+    split_rows = out_weight.shape[0] // 2
+    own_part = lax.dynamic_slice_in_dim(out_weight, half_index * split_rows, split_rows, 0)
+    gathered_part = lax.all_gather(own_part, "req", axis=0, tiled=False)
+    partner_part = lax.ppermute(gathered_part, "cfg", xor_pairs("cfg", 1))
+    every_weight = jnp.concatenate(
+        [
+            jnp.where(cond_first, gathered_part, partner_part),
+            jnp.where(cond_first, partner_part, gathered_part),
+        ],
+        axis=1,
+    )
+    half_values = latent.shape[2]
+    partner_latent = lax.ppermute(latent, "cfg", xor_pairs("cfg", 1))
+    full_latent = jnp.concatenate(
+        [
+            jnp.where(cond_first, latent, partner_latent),
+            jnp.where(cond_first, partner_latent, latent),
+        ],
+        axis=2,
+    )
     current, upcoming = plan(timestep)
     activated = jax.nn.silu(pooled[0] + time_features(current)).astype(jnp.bfloat16)
     columns = jnp.dot(activated, mod_weight, preferred_element_type=jnp.float32) + mod_bias
@@ -140,13 +162,12 @@
         live_keys,
     ).reshape(seq_count, row_count, head_width)
     attended_rows = lax.all_to_all(attended, "seq", 0, 0, tiled=True)
-    partial = jnp.einsum(
-        "rnk,kd->rnd", attended_rows, out_weight, preferred_element_type=jnp.float32
-    ).astype(jnp.bfloat16)
-    head_terms = lax.all_to_all(
-        partial.reshape(req_count, group_size, row_count, D), "req", 0, 0, tiled=True
-    )
-    attn_out = jnp.sum(head_terms.astype(jnp.float32), axis=0)
+    head_columns = lax.all_to_all(
+        attended_rows.reshape(req_count, group_size, row_count, head_width), "req", 0, 0, tiled=True
+    )
+    attn_out = jnp.einsum(
+        "grnk,gkd->rnd", head_columns, every_weight, preferred_element_type=jnp.float32
+    )
     img_mid = img_float + gate_attn * attn_out
     mlp_in = (layer_norm(img_mid) * (1.0 + scale_mlp) + shift_mlp).astype(jnp.bfloat16)
     all_rows = gather_by_a2a(mlp_in, "seq")
@@ -162,28 +183,23 @@
     own_velocity = jnp.einsum(
         "rnd,dc->rnc", final_in, final_weight, preferred_element_type=jnp.float32
     )
-    half_values = latent.shape[2]
-    half_index = lax.axis_index("cfg")
-    kept_velocity = lax.dynamic_slice_in_dim(own_velocity, half_index * half_values, half_values, 2)
-    sent_velocity = lax.dynamic_slice_in_dim(
-        own_velocity, (1 - half_index) * half_values, half_values, 2
-    )
-    other_velocity = lax.ppermute(sent_velocity, "cfg", xor_pairs("cfg", 1))
-    cond_first = half_index == 0
-    conditional = jnp.where(cond_first, kept_velocity, other_velocity)
-    unconditional = jnp.where(cond_first, other_velocity, kept_velocity)
+    other_velocity = lax.ppermute(own_velocity, "cfg", xor_pairs("cfg", 1))
+    conditional = jnp.where(cond_first, own_velocity, other_velocity)
+    unconditional = jnp.where(cond_first, other_velocity, own_velocity)
     guided = unconditional + GUIDANCE * (conditional - unconditional)
     offset = lax.axis_index("req") * group_size
     step_size = lax.dynamic_slice_in_dim(upcoming - current, offset, group_size, 0)
-    next_latent = latent + step_size[:, None, None] * guided
+    next_latent = full_latent + step_size[:, None, None] * guided
     squares = jnp.sum(next_latent * next_latent, axis=(1, 2))
     largest = jnp.max(jnp.abs(next_latent), axis=(1, 2))
-    for axis, distance in (("seq", 1), ("seq", 2), ("seq", 4), ("seq", 8), ("cfg", 1)):
-        if distance >= lax.axis_size(axis):
-            continue
-        stats = lax.ppermute(jnp.stack([squares, largest]), axis, xor_pairs(axis, distance))
+    distance = 1
+    while distance < seq_count:
+        stats = lax.ppermute(jnp.stack([squares, largest]), "seq", xor_pairs("seq", distance))
         squares = squares + stats[0]
         largest = jnp.maximum(largest, stats[1])
+        distance *= 2
+    guided = lax.dynamic_slice_in_dim(guided, half_index * half_values, half_values, 2)
+    next_latent = lax.dynamic_slice_in_dim(next_latent, half_index * half_values, half_values, 2)
     latent_norm = jnp.sqrt(squares / (IMG * PATCHC))
     return (guided, next_latent, latent_norm, largest)
 

time: 299 us -> 307 us (1.027); the launches traced: 298 us -> 303 us
  blocking collectives: 100 us -> 37.9 us
  waiting for transfers between devices: 104 us -> 134 us
  between operations: 1.15 us -> 14.5 us
  starting transfers between devices: 44.1 us -> 56.2 us
  local copies, waits for them, and re-layouts: 13.5 us -> 20 us
  matrix products: 19.8 us -> 23.7 us
    all_to_all x1 -> x2, waiting for transfers between devices: 6.83 us -> 71.7 us  [gather_by_a2a(): return lax.all_to_all(copies, axis, 0, 0, tiled=True)]
    all_to_all x2 -> x1, blocking collectives: 90 us -> 37.9 us  [gather_by_a2a(): return lax.all_to_all(copies, axis, 0, 0, tiled=True)]
    all_to_all x1 -> x2, waiting for transfers between devices: 36.4 us -> 12 us  [the longest x1 7.52 us: on_device(): attended_rows = lax.all_to_all(attended, 'seq', 0, 0, tiled=True)]
    all_to_all x1 -> x0, blocking collectives: 10.1 us -> none  [on_device(): attended_rows = lax.all_to_all(attended, 'seq', 0, 0, tiled=True)]
    all_to_all x1, waiting for transfers between devices: 35.7 us -> 29.1 us  [on_device(): block_terms = lax.all_to_all(mlp_terms, 'seq', 0, 0, tiled=True)]
    ppermute x6 -> x7, starting transfers between devices: 13.8 us -> 19.3 us  [the longest x1 8.6 us: on_device(): other_velocity = lax.ppermute(own_velocity, 'cfg', xor_pairs('cfg', 1))]
    select_n x0 -> x2, other arithmetic: none -> 4.89 us  [the longest x1 4.89 us: on_device(): jnp.where(cond_first, gathered_part, partner_part)]
    all_to_all x1 -> x2, starting transfers between devices: 6.75 us -> 11.2 us  [gather_by_a2a(): return lax.all_to_all(copies, axis, 0, 0, tiled=True)]
  transfers between devices with their start and end apart: 11 -> 15, of which waited for: 11 -> 12; matrix products, arithmetic and copies ran while one was open for 2% -> 13% of each run, Pallas kernels for 0% -> 0%
where the time goes in v2:
time: 307 us; the launch traced here: 303 us
  waiting for transfers between devices  134 us (44%)
  starting transfers between devices  56.2 us (18%)
  blocking collectives  37.9 us (12%)
  matrix products  23.7 us (8%)
  local copies, waits for them, and re-layouts  20 us (7%)
  other arithmetic  16.9 us (6%)
  between operations  14.5 us (5%)
    all_to_all x2, waiting for transfers between devices, gather_by_a2a(): return lax.all_to_all(copies, axis, 0, 0, tiled=True)  71.7 us
    all_to_all x1, blocking collectives, gather_by_a2a(): return lax.all_to_all(copies, axis, 0, 0, tiled=True)  37.9 us
    all_to_all x1, waiting for transfers between devices, on_device(): block_terms = lax.all_to_all(mlp_terms, 'seq', 0, 0, tiled=True)  29.1 us
    all_to_all x2, starting transfers between devices, gather_by_a2a(): return lax.all_to_all(copies, axis, 0, 0, tiled=True)  11.2 us
    ppermute x4, waiting for transfers between devices, on_device(): lax.ppermute(jnp.stack([squares, largest]), 'seq', xor_pairs('seq', dista...  10.4 us
    all_to_all x1, starting transfers between devices, on_device(): lax.all_to_all(columns.reshape(req_count, group_size, block_width), 'req'...  9 us
    ppermute x1, starting transfers between devices, on_device(): other_velocity = lax.ppermute(own_velocity, 'cfg', xor_pairs('cfg', 1))  8.6 us
    all_to_all x1, waiting for transfers between devices, on_device(): attended_rows = lax.all_to_all(attended, 'seq', 0, 0, tiled=True)  7.52 us
  transfers between devices with their start and end apart: 15, of which 12 were waited for; matrix products, arithmetic and copies ran while one was open for 13% of the time, Pallas kernels for 0%

profile of v2, /device:TPU:1, one launch (start us, length us, event | category | flops | bytes accessed | tf_op | source)
XLA Modules:
  0.0 302.9 jit_solution(3258330892542563386)
XLA Ops:
  7.2 0.8 divide_subtract_fusion
  8.3 1.8 convolution_add_fusion
  10.1 9.0 %all-to-all-start = ((f32[8,2,120]{2,1,0:T(2,128)}), f32[8,2,120]{2,1,0:T(2,128)S(1)}, u32[]{:S(2)}, u32[]{:S(2)}) async-start(f32[8,2,120]{2,1,0:T(2,128)} %bitcast.2), calls=%async_computation | async-start | bytes 16384 | tf_op jit(solution)/shard_map/all_to_all | solution.py:113
  19.1 1.0 convert_reduce_fusion.1
  20.2 1.1 fusion.39
  21.3 0.9 convert_reduce_fusion.2
  22.2 1.0 fusion.46
  23.2 2.5 all-to-all-done
  26.4 6.8 %all-to-all-start.1 = ((f32[16,8,2,120]{3,1,2,0:T(8,128)}), f32[16,8,2,120]{3,1,2,0:T(8,128)S(1)}, u32[]{:S(2)}, u32[]{:S(2)}) async-start(f32[16,8,2,120]{3,1,2,0:T(8,128)} %broadcast_in_dim.14), calls=%async_computation.1 | async-start | bytes 262144 | tf_op jit(solution)/shard_map/all_to_all | solution.py:51
  33.1 6.8 %all-to-all-done.1 = f32[16,8,2,120]{3,1,2,0:T(8,128)S(1)} async-done(((f32[16,8,2,120]{3,1,2,0:T(8,128)}), f32[16,8,2,120]{3,1,2,0:T(8,128)S(1)}, u32[]{:S(2)}, u32[]{:S(2)}) %all-to-all-start.1) | async-done | bytes 122912 | tf_op jit(solution)/shard_map/all_to_all | solution.py:51
  40.9 2.4 broadcast_in_dim.15
  43.3 4.5 %all-to-all-start.2 = ((bf16[8,2,42,1536]{3,1,2,0:T(2,128)(2,1)}), bf16[8,2,42,1536]{3,1,2,0:T(2,128)(2,1)}, u32[]{:S(2)}, u32[]{:S(2)}) async-start(bf16[8,2,42,1536]{3,1,2,0:T(2,128)(2,1)} %broadcast_in_dim.15), calls=%async_computation.2 | async-start | bytes 4128768 | tf_op jit(solution)/shard_map/all_to_all | solution.py:51
  48.7 64.9 %all-to-all-done.2 = bf16[8,2,42,1536]{3,1,2,0:T(2,128)(2,1)} async-done(((bf16[8,2,42,1536]{3,1,2,0:T(2,128)(2,1)}), bf16[8,2,42,1536]{3,1,2,0:T(2,128)(2,1)}, u32[]{:S(2)}, u32[]{:S(2)}) %all-to-all-start.2) | async-done | bytes 2064416 | tf_op jit(solution)/shard_map/all_to_all | solution.py:51
  113.5 2.0 copy.51
  115.6 1.4 copy-done.1
  117.0 1.4 fusion.20
  118.4 0.8 reshape.171
  119.2 2.1 convolution_convert_fusion.1
  121.9 1.2 reduce.2
  123.1 1.1 reshape.189
  124.2 4.3 %all-to-all-start.3 = ((bf16[16,2,11136]{2,1,0:T(2,128)(2,1)}), bf16[16,2,11136]{2,1,0:T(2,128)(2,1)}, u32[]{:S(2)}, u32[]{:S(2)}) async-start(bf16[16,2,11136]{2,1,0:T(2,128)(2,1)} %reshape.189), calls=%async_computation.3 | async-start | bytes 1425408 | tf_op jit(solution)/shard_map/all_to_all | solution.py:147
  128.5 2.8 collective-permute-start
  132.5 7.2 %all-to-all-done.3 = bf16[16,2,11136]{2,1,0:T(2,128)(2,1)} async-done(((bf16[16,2,11136]{2,1,0:T(2,128)(2,1)}), bf16[16,2,11136]{2,1,0:T(2,128)(2,1)}, u32[]{:S(2)}, u32[]{:S(2)}) %all-to-all-start.3) | async-done | bytes 712736 | tf_op jit(solution)/shard_map/all_to_all | solution.py:147
  139.7 4.2 %reshape.190 = bf16[16,1,22272]{2,1,0:T(2,128)(2,1)S(1)} reshape(bf16[16,2,11136]{2,1,0:T(2,128)(2,1)} %all-to-all-done.3) | data formatting | bytes 1425408
  144.0 0.8 reshape.174
  145.5 0.8 copy.55
  146.5 4.5 %fusion.72 = (f32[3,512]{1,0:T(4,128)S(1)}, f32[3,512,672]{1,2,0:T(8,128)}) fusion(pred[672]{0:T(1024)(128)(4,1)S(1)} %iota_compare_fusion, bf16[512,3,64]{0,2,1:T(8,128)(2,1)} %bitcast.178, bf16[672,3,64]{0,2,1:T(8,128)(2,1)S(1)} %bitcast.176), kind=kOutput, calls=%fused_computation.151 | convolution fusion | flops 136250016 | bytes 4590240 | tf_op jit(solution)/shard_map/sub | solution.py:62
  151.0 2.7 fusion.26
  154.0 1.0 reshape.179
  155.0 4.4 %all-to-all-start.4 = ((bf16[16,32,192]{2,1,0:T(8,128)(2,1)}), bf16[16,32,192]{2,1,0:T(8,128)(2,1)}, u32[]{:S(2)}, u32[]{:S(2)}) async-start(bf16[16,32,192]{2,1,0:T(8,128)(2,1)} %reshape.179), calls=%async_computation.4 | async-start | bytes 524288 | tf_op jit(solution)/shard_map/all_to_all | solution.py:164
  159.5 7.5 %all-to-all-done.4 = bf16[16,32,192]{2,1,0:T(8,128)(2,1)} async-done(((bf16[16,32,192]{2,1,0:T(8,128)(2,1)}), bf16[16,32,192]{2,1,0:T(8,128)(2,1)}, u32[]{:S(2)}, u32[]{:S(2)}) %all-to-all-start.4) | async-done | bytes 196640 | tf_op jit(solution)/shard_map/all_to_all | solution.py:164
  167.0 3.4 %all-to-all-start.5 = ((bf16[8,2,32,192]{3,2,1,0:T(8,128)(2,1)}), bf16[8,2,32,192]{3,2,1,0:T(8,128)(2,1)S(1)}, u32[]{:S(2)}, u32[]{:S(2)}) async-start(bf16[8,2,32,192]{3,2,1,0:T(8,128)(2,1)} %bitcast.16), calls=%async_computation.5 | async-start | bytes 524288 | tf_op jit(solution)/shard_map/all_to_all | solution.py:165
  170.4 4.9 %broadcast_select_fusion.1 = (bf16[8,96,1536]{2,1,0:T(8,128)(2,1)}, bf16[8,96,1536]{2,1,0:T(8,128)(2,1)}) fusion(bf16[8,96,1536]{2,1,0:T(8,128)(2,1)} %bitcast.173, bf16[8,96,1536]{2,1,0:T(8,128)(2,1)} %collective-permute-done, pred[]{:T(512)S(6)} %eq.3), kind=kLoop, calls=%fused_computation.11 | loop fusion | flops 2359296 | bytes 9437185 | tf_op jit(solution)/shard_map/jit(_where)/select_n | solution.py:95
  175.3 4.4 %all-to-all-done.5 = bf16[8,2,32,192]{3,2,1,0:T(8,128)(2,1)S(1)} async-done(((bf16[8,2,32,192]{3,2,1,0:T(8,128)(2,1)}), bf16[8,2,32,192]{3,2,1,0:T(8,128)(2,1)S(1)}, u32[]{:S(2)}, u32[]{:S(2)}) %all-to-all-start.5) | async-done | bytes 196640 | tf_op jit(solution)/shard_map/all_to_all | solution.py:165
  179.7 3.4 %fusion.73 = (f32[2,32]{1,0:T(2,128)S(1)}, f32[2,32,1536]{2,1,0:T(8,128)S(1)}) fusion(bf16[8,2,32,192]{3,2,1,0:T(8,128)(2,1)S(1)} %all-to-all-done.5, bf16[8,96,1536]{2,1,0:T(8,128)(2,1)} %get-tuple-element.13, bf16[8,96,1536]{2,1,0:T(8,128)(2,1)} %get-tuple-element.12, f32[2,1536]{1,0:T(2,128)S(1)} %bitcast.181, bf16[1,2,32,1536]{3,2,1,0:T(8,128)(2,1)S(1)} %copy-done.2), kind=kOutput, calls=%fused_computation.152 | convolution fusion | flops 311820224 | bytes 5517568 | tf_op jit(solution)/shard_map/grnk,gkd->rnd/dot_general | solution.py:168
  183.9 37.9 %all_to_all.47 = bf16[16,2,32,1536]{3,2,1,0:T(8,128)(2,1)} all-to-all(bf16[16,2,32,1536]{3,2,1,0:T(8,128)(2,1)S(1)} %broadcast_in_dim.18), channel_id=1, replica_groups=mesh['cfg'=2,'req'=8,'seq'=16] {'seq'}, dimensions={0} | all-to-all | bytes 6291456 | tf_op jit(solution)/shard_map/all_to_all | solution.py:51
  221.8 7.5 %convolution_convert_fusion = bf16[16,2,32,1536]{3,2,1,0:T(8,128)(2,1)} fusion(bf16[384,1536]{1,0:T(8,128)(2,1)S(1)} %copy-done.7, bf16[16,2,32,1536]{3,2,1,0:T(8,128)(2,1)} %all_to_all.47, bf16[1536,384]{1,0:T(8,128)(2,1)} %param.25), kind=kOutput, calls=%fused_computation.7 | convolution fusion | flops 2421030912 | bytes 8650752 | tf_op jit(solution)/shard_map/srnf,fd->srnd/dot_general | solution.py:176
  229.3 4.6 %all-to-all-start.7 = ((bf16[16,2,32,1536]{3,2,1,0:T(8,128)(2,1)}), bf16[16,2,32,1536]{3,2,1,0:T(8,128)(2,1)}, u32[]{:S(2)}, u32[]{:S(2)}) async-start(bf16[16,2,32,1536]{3,2,1,0:T(8,128)(2,1)} %convolution_convert_fusion), calls=%async_computation.7 | async-start | bytes 6291456 | tf_op jit(solution)/shard_map/all_to_all | solution.py:179
  233.9 6.6 %collective-permute-start.2 = (f32[2,32,32]{2,1,0:T(8,128)S(1)}, f32[2,32,32]{2,1,0:T(8,128)S(1)}, u32[]{:S(2)}, u32[]{:S(2)}) collective-permute-start(f32[2,32,32]{2,1,0:T(8,128)S(1)} %copy-done.6), channel_id=1, source_target_pairs={{0,128},{128,0},{1,129},{129,1},{2,130},{130,2},{3,131},{131,3},{4... | collective-permute-start | bytes 24584 | tf_op jit(solution)/shard_map/ppermute | solution.py:101
  240.6 29.1 %all-to-all-done.7 = bf16[16,2,32,1536]{3,2,1,0:T(8,128)(2,1)} async-done(((bf16[16,2,32,1536]{3,2,1,0:T(8,128)(2,1)}), bf16[16,2,32,1536]{3,2,1,0:T(8,128)(2,1)}, u32[]{:S(2)}, u32[]{:S(2)}) %all-to-all-start.7) | async-done | bytes 3145760 | tf_op jit(solution)/shard_map/all_to_all | solution.py:179
  269.7 2.4 convert_reduce_fusion
  272.8 8.6 %collective-permute-start.1 = (f32[2,32,64]{2,1,0:T(8,128)S(1)}, f32[2,32,64]{2,1,0:T(8,128)S(1)}, u32[]{:S(2)}, u32[]{:S(2)}) collective-permute-start(f32[2,32,64]{2,1,0:T(8,128)S(1)} %fusion.50), channel_id=1, source_target_pairs={{0,128},{128,0},{1,129},{129,1},{2,130},{130,2},{3,131},{131,3},{4... | collective-permute-start | bytes 49160 | tf_op jit(solution)/shard_map/ppermute | solution.py:186
  281.4 0.8 collective-permute-done.1
  283.9 1.0 collective-permute-done.3
  285.0 3.9 %collective-permute-done.4 = f32[2,2]{1,0:T(2,128)S(1)} collective-permute-done((f32[2,2]{1,0:T(2,128)S(1)}, f32[2,2]{1,0:T(2,128)S(1)}, u32[]{:S(2)}, u32[]{:S(2)}) %collective-permute-start.4) | collective-permute-done | bytes 48 | tf_op jit(solution)/shard_map/ppermute | solution.py:197
  289.1 2.4 collective-permute-done.5
  291.5 1.0 collective-permute-start.6
  292.5 3.0 collective-permute-done.6
  (87 shorter events, 9.6 us)
Async XLA Ops:
  7.2 108.4 %copy-start = (bf16[1536,3,192]{0,2,1:T(8,128)(2,1)S(1)}, bf16[1536,3,192]{0,2,1:T(8,128)(2,1)}, u32[]{:S(2)}) copy-start(bf16[1536,3,192]{0,2,1:T(8,128)(2,1)} %param.22) | copy-start | bytes 5308420
  7.2 33.1 %copy-start.2 = (bf16[1,2,32,1536]{3,2,1,0:T(8,128)(2,1)S(1)}, bf16[1,2,32,1536]{3,2,1,0:T(8,128)(2,1)}, u32[]{:S(2)}) copy-start(bf16[1,2,32,1536]{3,2,1,0:T(8,128)(2,1)} %param.14) | copy-start | bytes 589828
  7.2 33.3 %copy-start.3 = (bf16[1,2,10,1536]{3,1,2,0:T(2,128)(2,1)S(1)}, bf16[1,2,10,1536]{3,1,2,0:T(2,128)(2,1)}, u32[]{:S(2)}) copy-start(bf16[1,2,10,1536]{3,1,2,0:T(2,128)(2,1)} %param.15) | copy-start | bytes 184324
  10.1 15.6 %all-to-all-start = ((f32[8,2,120]{2,1,0:T(2,128)}), f32[8,2,120]{2,1,0:T(2,128)S(1)}, u32[]{:S(2)}, u32[]{:S(2)}) async-start(f32[8,2,120]{2,1,0:T(2,128)} %bitcast.2), calls=%async_computation | async-start | bytes 16384 | tf_op jit(solution)/shard_map/all_to_all | solution.py:113
  26.4 13.6 %all-to-all-start.1 = ((f32[16,8,2,120]{3,1,2,0:T(8,128)}), f32[16,8,2,120]{3,1,2,0:T(8,128)S(1)}, u32[]{:S(2)}, u32[]{:S(2)}) async-start(f32[16,8,2,120]{3,1,2,0:T(8,128)} %broadcast_in_dim.14), calls=%async_computation.1 | async-start | bytes 262144 | tf_op jit(solution)/shard_map/all_to_all | solution.py:51
  43.3 4.6 %copy-start.5 = (bf16[192,1536]{1,0:T(8,128)(2,1)S(1)}, bf16[192,1536]{1,0:T(8,128)(2,1)}, u32[]{:S(2)}) copy-start(bf16[192,1536]{1,0:T(8,128)(2,1)} %param.24) | copy-start | bytes 1769476
  43.3 70.2 %all-to-all-start.2 = ((bf16[8,2,42,1536]{3,1,2,0:T(2,128)(2,1)}), bf16[8,2,42,1536]{3,1,2,0:T(2,128)(2,1)}, u32[]{:S(2)}, u32[]{:S(2)}) async-start(bf16[8,2,42,1536]{3,1,2,0:T(2,128)(2,1)} %broadcast_in_dim.15), calls=%async_computation.2 | async-start | bytes 4128768 | tf_op jit(solution)/shard_map/all_to_all | solution.py:51
  47.8 80.6 %all-gather.3.cloned.1.call-start = ((), (), s32[]{:S(2)}) async-start(), calls=%async_computation.8 | async-start | bytes 2654208 | tf_op jit(solution)/shard_map/all_gather | solution.py:91
  115.5 1.4 copy-start.1
  121.4 9.9 %copy-start.8 = (s32[1,16]{1,0:T(1,128)S(1)}, s32[1,16]{1,0:T(1,128)}, u32[]{:S(2)}) copy-start(s32[1,16]{1,0:T(1,128)} %param.16) | copy-start | bytes 196
  124.2 15.6 %all-to-all-start.3 = ((bf16[16,2,11136]{2,1,0:T(2,128)(2,1)}), bf16[16,2,11136]{2,1,0:T(2,128)(2,1)}, u32[]{:S(2)}, u32[]{:S(2)}) async-start(bf16[16,2,11136]{2,1,0:T(2,128)(2,1)} %reshape.189), calls=%async_computation.3 | async-start | bytes 1425408 | tf_op jit(solution)/shard_map/all_to_all | solution.py:147
  128.5 41.9 %collective-permute-start = (bf16[8,96,1536]{2,1,0:T(8,128)(2,1)}, bf16[8,96,1536]{2,1,0:T(8,128)(2,1)}, u32[]{:S(2)}, u32[]{:S(2)}) collective-permute-start(bf16[8,96,1536]{2,1,0:T(8,128)(2,1)} %bitcast.172), channel_id=1, source_target_pairs={{0,128},{128,0},{1,129},{129,1},{2,130},{130,2},{3,131},{131,3},{4... | collective-permute-start | bytes 7077896 | tf_op jit(solution)/shard_map/ppermute | solution.py:92
  155.0 11.9 %all-to-all-start.4 = ((bf16[16,32,192]{2,1,0:T(8,128)(2,1)}), bf16[16,32,192]{2,1,0:T(8,128)(2,1)}, u32[]{:S(2)}, u32[]{:S(2)}) async-start(bf16[16,32,192]{2,1,0:T(8,128)(2,1)} %reshape.179), calls=%async_computation.4 | async-start | bytes 524288 | tf_op jit(solution)/shard_map/all_to_all | solution.py:164
  167.0 12.8 %all-to-all-start.5 = ((bf16[8,2,32,192]{3,2,1,0:T(8,128)(2,1)}), bf16[8,2,32,192]{3,2,1,0:T(8,128)(2,1)S(1)}, u32[]{:S(2)}, u32[]{:S(2)}) async-start(bf16[8,2,32,192]{3,2,1,0:T(8,128)(2,1)} %bitcast.16), calls=%async_computation.5 | async-start | bytes 524288 | tf_op jit(solution)/shard_map/all_to_all | solution.py:165
  183.9 37.9 %copy-start.7 = (bf16[384,1536]{1,0:T(8,128)(2,1)S(1)}, bf16[384,1536]{1,0:T(8,128)(2,1)}, u32[]{:S(2)}) copy-start(bf16[384,1536]{1,0:T(8,128)(2,1)} %param.26) | copy-start | bytes 3538948
  229.3 4.6 %copy-start.6 = (f32[2,32,32]{2,1,0:T(8,128)S(1)}, f32[2,32,32]{2,1,0:T(8,128)}, u32[]{:S(2)}) copy-start(f32[2,32,32]{2,1,0:T(8,128)} %param.19) | copy-start | bytes 24580
  229.3 40.5 %all-to-all-start.7 = ((bf16[16,2,32,1536]{3,2,1,0:T(8,128)(2,1)}), bf16[16,2,32,1536]{3,2,1,0:T(8,128)(2,1)}, u32[]{:S(2)}, u32[]{:S(2)}) async-start(bf16[16,2,32,1536]{3,2,1,0:T(8,128)(2,1)} %convolution_convert_fusion), calls=%async_computation.7 | async-start | bytes 6291456 | tf_op jit(solution)/shard_map/all_to_all | solution.py:179
  233.9 47.4 %collective-permute-start.2 = (f32[2,32,32]{2,1,0:T(8,128)S(1)}, f32[2,32,32]{2,1,0:T(8,128)S(1)}, u32[]{:S(2)}, u32[]{:S(2)}) collective-permute-start(f32[2,32,32]{2,1,0:T(8,128)S(1)} %copy-done.6), channel_id=1, source_target_pairs={{0,128},{128,0},{1,129},{129,1},{2,130},{130,2},{3,131},{131,3},{4... | collective-permute-start | bytes 24584 | tf_op jit(solution)/shard_map/ppermute | solution.py:101
  240.6 31.9 %copy-start.4 = (bf16[1536,64]{0,1:T(8,128)(2,1)S(1)}, bf16[1536,64]{0,1:T(8,128)(2,1)}, u32[]{:S(2)}) copy-start(bf16[1536,64]{0,1:T(8,128)(2,1)} %param.27) | copy-start | bytes 589828
  272.8 9.5 %collective-permute-start.1 = (f32[2,32,64]{2,1,0:T(8,128)S(1)}, f32[2,32,64]{2,1,0:T(8,128)S(1)}, u32[]{:S(2)}, u32[]{:S(2)}) collective-permute-start(f32[2,32,64]{2,1,0:T(8,128)S(1)} %fusion.50), channel_id=1, source_target_pairs={{0,128},{128,0},{1,129},{129,1},{2,130},{130,2},{3,131},{131,3},{4... | collective-permute-start | bytes 49160 | tf_op jit(solution)/shard_map/ppermute | solution.py:186
  282.4 2.5 collective-permute-start.3
  284.9 4.0 %collective-permute-start.4 = (f32[2,2]{1,0:T(2,128)S(1)}, f32[2,2]{1,0:T(2,128)S(1)}, u32[]{:S(2)}, u32[]{:S(2)}) collective-permute-start(f32[2,2]{1,0:T(2,128)S(1)} %pad_maximum_fusion.4), channel_id=1, source_target_pairs={{0,2},{1,3},{2,0},{3,1},{4,6},{5,7},{6,4},{7,5},{8,10},{9,11},{10,... | collective-permute-start | bytes 56 | tf_op jit(solution)/shard_map/ppermute | solution.py:197
  289.0 2.5 collective-permute-start.5
  291.5 4.0 %collective-permute-start.6 = (f32[2,2]{1,0:T(2,128)S(1)}, f32[2,2]{1,0:T(2,128)S(1)}, u32[]{:S(2)}, u32[]{:S(2)}) collective-permute-start(f32[2,2]{1,0:T(2,128)S(1)} %pad_maximum_fusion.6), channel_id=1, source_target_pairs={{0,8},{1,9},{2,10},{3,11},{4,12},{5,13},{6,14},{7,15},{8,0},{9,1},... | collective-permute-start | bytes 56 | tf_op jit(solution)/shard_map/ppermute | solution.py:197
Sparse Core Ops, SparseCore 0:
  50.4 67.7 all-gather.2
